TPU v7x, 256 devices: a whole 4x4x8 slice. The times are simulated.
256 devices in a mesh: dp: 32 (over y, z), tensor: 8 (over x, core).
Axes of the slice: x: 4, y: 4, z: 8, core: 2. Of those that a mesh axis runs over, the one named last changes fastest.
Arguments:
- residual_in: bfloat16 [2048, 2048], P(('dp', 'tensor')), may hold values from -6 to 6
- attn_gain: float32 [2048], replicated, may hold values from 0.5 to 1.5
- query_weight: bfloat16 [2048, 4096], P(None, 'tensor'), may hold values from -0.125 to 0.125
- kv_weight: bfloat16 [2048, 1024], P(None, 'tensor'), may hold values from -0.125 to 0.125
- query_gain: float32 [128], replicated, may hold values from 0.25 to 1.75
- key_gain: float32 [128], replicated, may hold values from 0.25 to 1.75
- out_weight: bfloat16 [4096, 2048], P('tensor'), may hold values from -0.09375 to 0.09375
- moe_gain: float32 [2048], replicated, may hold values from 0.5 to 1.5
- gate_weight: bfloat16 [128, 2048, 768], P('dp', None, 'tensor'), may hold values from -0.1875 to 0.1875
- lift_weight: bfloat16 [128, 2048, 768], P('dp', None, 'tensor'), may hold values from -0.1875 to 0.1875
- down_weight: bfloat16 [128, 768, 2048], P('dp', 'tensor'), may hold values from -0.21875 to 0.21875
- routes: int32 [2048, 8], P('dp'), may hold values from 0 to 127, as said below
- route_weights: float32 [2048, 8], P('dp'), may hold values from 0.5 to 1
- prefix_cache: bfloat16 [64, 2048, 1024], P('dp', 'tensor'), may hold values from -250 to 250
- suffix_cache: bfloat16 [2048, 128, 1024], P('dp', 'tensor'), may hold values from -250 to 250
- prefix_len: int32 [64], P('dp'), may hold values from 1 to 2048, as said below
- suffix_len: int32 [2048], P('dp'), may hold values from 1 to 128, as said below
- request_group: int32 [2048], P('dp'), may hold values from 0 to 63, as said below
Outputs:
- layer_out: bfloat16 [2048, 2048], P(('dp', 'tensor'))
- new_cache_rows: bfloat16 [2048, 1024], P('dp', 'tensor')
Inputs may be any that keep to these rules, and one draw needn't show every extreme that they name: `routes`: each block of 64 rows (the requests of one index of dp) names 64 of the experts exactly 8 times each and no other expert; one expert is among them in every block. `request_group`: request r belongs to one of the groups (r // 64) * 2 to (r // 64) * 2 + 1. `prefix_len`: some shared prompt has all 2048 slots live. `suffix_len`: some request has all 128 suffix slots live.
All inputs are finite; a program needn't handle non-finite values.
Results may differ from a plain program's by a relative error of at most 0.02.
Values may be sent and summed in bfloat16 or wider, within the bound.
No kernel may reach another device: no remote copies, remote signals or barrier semaphores. Data moves between devices by JAX's collectives and lax.ppermute only.
A program may use at most 128 MiB of HBM per device.

v0:
```python
import math
import jax
import jax.numpy as jnp
from jax import lax
from jax.sharding import Mesh, PartitionSpec as P

EPSILON = 1e-06
THETA = 1000000.0
NEGATIVE = -1e30
TENSOR = ("tx", "tc")


def rms_scale(values, gain):
    mean_square = jnp.mean(values * values, axis=-1, keepdims=True)
    return values * lax.rsqrt(mean_square + EPSILON) * gain


def rotate(values, positions):
    half = values.shape[-1] // 2
    freqs = THETA ** (-jnp.arange(half).astype(jnp.float32) * 2.0 / values.shape[-1])
    angles = positions.astype(jnp.float32)[:, None] * freqs[None, :]
    angles = jnp.concatenate([angles, angles], axis=-1)
    cosine = jnp.cos(angles)[:, None, :]
    sine = jnp.sin(angles)[:, None, :]
    turned = jnp.concatenate([-values[..., half:], values[..., :half]], axis=-1)
    return values * cosine + turned * sine


def body(
    residual_in,
    attn_gain,
    query_weight,
    kv_weight,
    query_gain,
    key_gain,
    out_weight,
    moe_gain,
    gate_weight,
    lift_weight,
    down_weight,
    routes,
    route_weights,
    prefix_cache,
    suffix_cache,
    prefix_len,
    suffix_len,
    request_group,
):
    tensor_size = lax.axis_size(TENSOR)
    chip_rank = lax.axis_index("tx")
    core_rank = lax.axis_index("tc")
    chips = lax.axis_size("tx")
    tensor_rank = chip_rank * lax.axis_size("tc") + core_rank
    chunk_rank = core_rank * chips + chip_rank
    dp_rank = lax.axis_index("dp")
    owners = lax.axis_size("dp")
    head_dim = query_gain.shape[0]
    requests = routes.shape[0]
    model_width = residual_in.shape[1]
    query_cols = query_weight.shape[1]
    kv_cols = kv_weight.shape[1]
    heads_here = query_cols // head_dim
    heads_all = heads_here * tensor_size
    kv_heads_all = kv_cols * tensor_size // (2 * head_dim)
    per_group = heads_all // kv_heads_all
    groups_dev = prefix_cache.shape[0]
    pre_local = prefix_cache.shape[1]
    suf_local = suffix_cache.shape[1]
    residual_all = lax.all_gather(residual_in, TENSOR, axis=0, tiled=True)
    piece = rms_scale(residual_all.astype(jnp.float32), attn_gain).astype(jnp.bfloat16)
    projected = jnp.concatenate(
        [
            jnp.dot(piece, query_weight, preferred_element_type=jnp.float32),
            jnp.dot(piece, kv_weight, preferred_element_type=jnp.float32),
        ],
        axis=1,
    )
    query_raw = projected[:, :query_cols].reshape(requests, heads_here, head_dim)
    kv_raw = projected[:, query_cols:].reshape(requests, kv_cols // head_dim, head_dim)
    group_ids = dp_rank * groups_dev + jnp.arange(groups_dev)
    member = request_group[:, None] == group_ids[None, :]
    prefix_of = jnp.sum(jnp.where(member, prefix_len[None, :], 0), axis=1)
    positions = prefix_of + suffix_len
    queries = rotate(rms_scale(query_raw, query_gain), positions).astype(jnp.bfloat16)
    head_number = tensor_rank * (kv_cols // head_dim) + jnp.arange(kv_cols // head_dim)
    is_key = (head_number < kv_heads_all)[None, :, None]
    keyed = rotate(rms_scale(kv_raw, key_gain), positions)
    new_rows = jnp.where(is_key, keyed, kv_raw).astype(jnp.bfloat16).reshape(requests, kv_cols)
    joined = jnp.concatenate([queries.reshape(requests, query_cols), new_rows], axis=1)
    every_head = lax.all_gather(joined, TENSOR, axis=1, tiled=True).reshape(
        requests, tensor_size, query_cols + kv_cols
    )
    all_queries = every_head[:, :, :query_cols].reshape(requests, kv_heads_all, per_group, head_dim)
    all_kv = every_head[:, :, query_cols:]
    own_keys = all_kv[:, :kv_heads_all]
    own_values = all_kv[:, kv_heads_all:].astype(jnp.float32)
    scale = 1.0 / math.sqrt(head_dim)
    split_at = kv_heads_all * head_dim
    pre_keys = prefix_cache[:, :, :split_at].reshape(groups_dev, pre_local, kv_heads_all, head_dim)
    pre_values = prefix_cache[:, :, split_at:].reshape(
        groups_dev, pre_local, kv_heads_all, head_dim
    )
    suf_keys = suffix_cache[:, :, :split_at].reshape(requests, suf_local, kv_heads_all, head_dim)
    suf_values = suffix_cache[:, :, split_at:].reshape(requests, suf_local, kv_heads_all, head_dim)
    pre_scores = (
        jnp.einsum("rgqd,npgd->rgqnp", all_queries, pre_keys, preferred_element_type=jnp.float32)
        * scale
    )
    suf_scores = (
        jnp.einsum("rgqd,rsgd->rgqs", all_queries, suf_keys, preferred_element_type=jnp.float32)
        * scale
    )
    own_scores = (
        jnp.einsum("rgqd,rgd->rgq", all_queries, own_keys, preferred_element_type=jnp.float32)
        * scale
    )
    pre_slots = tensor_rank * pre_local + jnp.arange(pre_local)
    pre_valid = (member[:, :, None] & (pre_slots[None, None, :] < prefix_len[None, :, None]))[
        :, None, None, :, :
    ]
    suf_slots = tensor_rank * suf_local + jnp.arange(suf_local)
    suf_valid = (suf_slots[None, :] < suffix_len[:, None])[:, None, None, :]
    own_valid = tensor_rank == 0
    top_pre = jnp.max(jnp.where(pre_valid, pre_scores, NEGATIVE), axis=(3, 4))
    top_suf = jnp.max(jnp.where(suf_valid, suf_scores, NEGATIVE), axis=3)
    top_own = jnp.where(own_valid, own_scores, NEGATIVE)
    top_local = jnp.maximum(jnp.maximum(top_pre, top_suf), top_own)
    pre_weights = jnp.where(pre_valid, jnp.exp(pre_scores - top_local[..., None, None]), 0.0)
    suf_weights = jnp.where(suf_valid, jnp.exp(suf_scores - top_local[..., None]), 0.0)
    own_weights = jnp.where(own_valid, jnp.exp(own_scores - top_local), 0.0)
    total_local = jnp.sum(pre_weights, axis=(3, 4)) + jnp.sum(suf_weights, axis=3) + own_weights
    sums_local = jnp.einsum(
        "rgqnp,npgd->rgqd",
        pre_weights.astype(jnp.bfloat16),
        pre_values,
        preferred_element_type=jnp.float32,
    )
    sums_local = sums_local + jnp.einsum(
        "rgqs,rsgd->rgqd",
        suf_weights.astype(jnp.bfloat16),
        suf_values,
        preferred_element_type=jnp.float32,
    )
    own_low = own_weights.astype(jnp.bfloat16).astype(jnp.float32)
    sums_local = sums_local + own_low[..., None] * own_values[:, :, None, :]
    packed = jnp.concatenate(
        [
            sums_local.reshape(requests, heads_all, head_dim),
            top_local.reshape(requests, heads_all, 1),
            total_local.reshape(requests, heads_all, 1),
        ],
        axis=2,
    )
    packed = packed.reshape(requests, tensor_size, heads_here, head_dim + 2).transpose(1, 0, 2, 3)
    parts = lax.all_to_all(packed, TENSOR, 0, 0, tiled=True)
    part_sums = parts[..., :head_dim]
    part_top = parts[..., head_dim]
    part_total = parts[..., head_dim + 1]
    top_all = jnp.max(part_top, axis=0)
    factor = jnp.exp(part_top - top_all[None])
    total_mine = jnp.sum(part_total * factor, axis=0)
    sums_mine = jnp.sum(part_sums * factor[..., None], axis=0)
    mixed = sums_mine / total_mine[..., None]
    attn_heads = mixed.reshape(requests, query_cols).astype(jnp.bfloat16)
    attn_all = lax.psum(jnp.dot(attn_heads, out_weight, preferred_element_type=jnp.float32), TENSOR)
    middle_all = (residual_all.astype(jnp.float32) + attn_all).astype(jnp.bfloat16)
    tokens_here = residual_in.shape[0]
    middle = lax.dynamic_slice_in_dim(middle_all, tensor_rank * tokens_here, tokens_here, 0)
    moe_all = rms_scale(middle_all.astype(jnp.float32), moe_gain).astype(jnp.bfloat16)
    local_experts = gate_weight.shape[0]
    experts_all = local_experts * owners
    topk = routes.shape[1]
    capacity = 2 * requests * topk // experts_all
    flat_routes = routes.reshape(-1)
    onehot = (flat_routes[:, None] == jnp.arange(experts_all)[None, :]).astype(jnp.int32)
    running = jnp.cumsum(onehot, axis=0)
    slot_of = jnp.sum(onehot * running, axis=1) - 1
    code_of = (flat_routes * capacity + slot_of).reshape(requests, topk)
    code_span = jnp.arange(experts_all * capacity)
    placing = jnp.any(code_of[None, :, :] == code_span[:, None, None], axis=2).astype(jnp.bfloat16)
    share = route_weights / jnp.sum(route_weights, axis=1, keepdims=True)
    width_here = model_width // tensor_size
    cols_in = lax.dynamic_slice_in_dim(moe_all, chunk_rank * width_here, width_here, 1)
    placed = jnp.dot(placing, cols_in, preferred_element_type=jnp.float32)
    outgoing = placed.astype(jnp.bfloat16).reshape(owners, local_experts * capacity, width_here)
    arrived = lax.all_to_all(outgoing, "dp", split_axis=0, concat_axis=0, tiled=True)
    half_rows = lax.all_gather(arrived, "tx", axis=2, tiled=True)
    rows = lax.all_gather(half_rows, "tc", axis=2, tiled=True).reshape(
        owners, local_experts, capacity, model_width
    )
    gate_val = jnp.einsum("necd,edf->necf", rows, gate_weight, preferred_element_type=jnp.float32)
    lift_val = jnp.einsum("necd,edf->necf", rows, lift_weight, preferred_element_type=jnp.float32)
    hidden_units = (jax.nn.silu(gate_val) * lift_val).astype(jnp.bfloat16)
    partial_out = jnp.einsum(
        "necf,efd->necd", hidden_units, down_weight, preferred_element_type=jnp.float32
    ).astype(jnp.bfloat16)
    core_out = lax.psum_scatter(partial_out, "tc", scatter_dimension=3, tiled=True)
    summed_out = lax.psum_scatter(core_out, "tx", scatter_dimension=3, tiled=True)
    returned = lax.all_to_all(
        summed_out.reshape(owners, local_experts * capacity, width_here),
        "dp",
        split_axis=0,
        concat_axis=0,
        tiled=True,
    ).astype(jnp.float32)
    returned = returned.reshape(experts_all * capacity, width_here)
    picked_rows = returned[code_of]
    moe_cols = jnp.sum(share[:, :, None] * picked_rows, axis=1).astype(jnp.bfloat16)
    moe_chunks = lax.all_to_all(moe_cols, TENSOR, split_axis=0, concat_axis=1, tiled=True)
    moe_out = (
        moe_chunks.reshape(tokens_here, chips, tensor_size // chips, width_here)
        .transpose(0, 2, 1, 3)
        .reshape(tokens_here, model_width)
        .astype(jnp.float32)
    )
    layer_out = (middle.astype(jnp.float32) + moe_out).astype(jnp.bfloat16)
    return (layer_out, new_rows)


def solution(mesh):
    cores = mesh.devices.shape[1] // 2
    split_mesh = Mesh(mesh.devices.reshape(mesh.devices.shape[0], cores, 2), ("dp", "tx", "tc"))
    in_specs = (
        P(("dp", "tx", "tc"), None),
        P(),
        P(None, TENSOR),
        P(None, TENSOR),
        P(),
        P(),
        P(TENSOR, None),
        P(),
        P("dp", None, TENSOR),
        P("dp", None, TENSOR),
        P("dp", TENSOR, None),
        P("dp", None),
        P("dp", None),
        P("dp", TENSOR, None),
        P("dp", TENSOR, None),
        P("dp"),
        P("dp"),
        P("dp"),
    )
    out_specs = (P(("dp", "tx", "tc"), None), P("dp", TENSOR))
    return jax.shard_map(
        body, mesh=split_mesh, in_specs=in_specs, out_specs=out_specs, check_vma=False
    )
```

profile of v0, /device:TPU:32, one launch (start us, length us, event | category | flops | bytes accessed | tf_op | source)
XLA Modules:
  0.0 390.6 jit_solution(887518312369594651)
XLA Ops:
  7.3 13.5 %all_gather.12 = bf16[64,2048]{1,0:T(8,128)(2,1)S(1)} all-gather(bf16[8,2048]{1,0:T(8,128)(2,1)} %param.18), channel_id=1, replica_groups=mesh['dp'=32,'tx'=4,'tc'=2] {'tx','tc'}, dimensions={0}, use_global_device_ids=true | all-gather | bytes 294912 | tf_op jit(solution)/shard_map/all_gather | solution.py:69
  23.2 2.1 fusion.80
  26.8 13.3 %all_gather.13 = bf16[64,5120]{1,0:T(8,128)(2,1)S(1)} all-gather(bf16[64,640]{1,0:T(8,128)(2,1)S(1)} %pad_maximum_fusion), channel_id=1, replica_groups=mesh['dp'=32,'tx'=4,'tc'=2] {'tx','tc'}, dimensions={1}, use_global_device_ids=true | all-gather | bytes 737280 | tf_op jit(solution)/shard_map/all_gather | solution.py:90
  42.0 2.1 fusion.107
  44.0 2.0 copy.308
  46.2 4.6 %fusion = (f32[64,4,8]{2,0,1:T(8,128)}, f32[4,64,8,2,256]{4,2,3,1,0:T(8,128)}) fusion(pred[64,2,256]{2,1,0:T(4,128)(4,1)S(1)} %broadcast_and_fusion, bf16[2,256,4,128,1]{1,3,2,0,4:T(8,128)(2,1)} %bitcast.194, bf16[64,4,8,128]{3,2,1,0:T(8,128)(2,1)S(1)} %reshape.329), kind=kOutput, calls=%fused_computation.3 | convolution fusion | flops 271579136 | bytes 5283840 | tf_op jit(solution)/shard_map/rgqd,npgd->rgqnp/dot_general | solution.py:106
  50.8 1.6 copy.258
  52.5 2.9 slice_bitcast_fusion
  55.4 2.4 select_reduce_fusion
  62.0 4.4 %fusion.7 = f32[64,4,8]{2,0,1:T(8,128)} fusion(f32[4,64,8,2,256]{4,2,3,1,0:T(8,128)} %get-tuple-element.29, f32[64,4,8]{2,0,1:T(8,128)S(1)} %copy.260, pred[64,2,256]{2,1,0:T(4,128)(4,1)S(1)} %broadcast_and_fusion), kind=kLoop, calls=%fused_computation.11 | loop fusion | flops 4192256 | bytes 4243456 | tf_op jit(solution)/shard_map/reduce_sum | solution.py:131
  66.5 3.2 fusion.19
  72.8 2.0 fusion.22
  80.3 3.3 maximum_bitcast_fusion
  83.5 4.3 %all-to-all-start = ((f32[8,64,4,130]{3,1,2,0:T(8,128)}), f32[8,64,4,130]{3,1,2,0:T(8,128)}, u32[]{:S(2)}, u32[]{:S(2)}) async-start(f32[8,64,4,130]{3,1,2,0:T(8,128)} %maximum_bitcast_fusion), calls=%async_computation | async-start | bytes 4194304 | tf_op jit(solution)/shard_map/all_to_all | solution.py:155
  89.2 25.8 %all-to-all-done = f32[8,64,4,130]{3,1,2,0:T(8,128)} async-done(((f32[8,64,4,130]{3,1,2,0:T(8,128)}), f32[8,64,4,130]{3,1,2,0:T(8,128)}, u32[]{:S(2)}, u32[]{:S(2)}) %all-to-all-start) | async-done | bytes 1064992 | tf_op jit(solution)/shard_map/all_to_all | solution.py:155
  115.0 3.0 fusion.106
  118.1 1.6 copy.311
  124.7 65.4 %all-reduce.2.cloned.1.call-done = f32[64,2048]{1,0:T(8,128)} async-done(((f32[64,2048]{1,0:T(8,128)}), f32[64,2048]{1,0:T(8,128)}) %all-reduce.2.cloned.1.call-update) | async-done | bytes 524304 | tf_op jit(solution)/shard_map/psum | solution.py:165
  192.4 25.5 %all_to_all.25 = bf16[32,32,256]{2,1,0:T(8,128)(2,1)} all-to-all(bf16[32,32,256]{2,1,0:T(8,128)(2,1)S(1)} %bitcast.193), channel_id=1, replica_groups=mesh['dp'=32,'tx'=4,'tc'=2] {'dp'}, dimensions={0} | all-to-all | bytes 1048576 | tf_op jit(solution)/shard_map/all_to_all | solution.py:186
  218.0 33.2 %all-gather.3.cloned.1.call-done = bf16[32,32,1024]{2,1,0:T(8,128)(2,1)} async-done(((bf16[32,32,256]{2,1,0:T(8,128)(2,1)}), bf16[32,32,1024]{2,1,0:T(8,128)(2,1)}) %all-gather.3.cloned.1.call-update) | async-done | bytes 2097168 | tf_op jit(solution)/shard_map/all_gather | solution.py:187
  251.3 21.8 %all-gather.5.cloned.1.call-done = bf16[32,32,2048]{2,1,0:T(8,128)(2,1)} async-done(((bf16[32,32,1024]{2,1,0:T(8,128)(2,1)}), bf16[32,32,2048]{2,1,0:T(8,128)(2,1)}) %all-gather.5.cloned.1.call-update) | async-done | bytes 4194320 | tf_op jit(solution)/shard_map/all_gather | solution.py:188
  273.0 3.9 %fusion.23 = f32[32,4,8,96]{3,2,0,1:T(8,128)S(1)} fusion(bf16[4,2048,96]{1,2,0:T(8,128)(2,1)} %param.26, bf16[32,32,2048]{2,1,0:T(8,128)(2,1)} %all-gather.5.cloned.1.call-done), kind=kOutput, calls=%fused_computation.29 | convolution fusion | flops 402653184 | bytes 6160384 | tf_op jit(solution)/shard_map/necd,edf->necf/dot_general | solution.py:191
  276.9 7.4 %convert_bitcast_fusion = bf16[32,4,8,2048]{3,2,0,1:T(8,128)(2,1)} fusion(bf16[4,96,2048]{2,1,0:T(8,128)(2,1)} %param.28, bf16[4,2048,96]{1,2,0:T(8,128)(2,1)} %param.27, f32[32,4,8,96]{3,2,0,1:T(8,128)S(1)} %fusion.23, bf16[32,32,2048]{2,1,0:T(8,128)(2,1)} %all-gather.5.cloned.1.call-done), kind=kOutput, calls=%fused_computation.6 | convolution fusion | flops 807993344 | bytes 11927552 | tf_op jit(solution)/shard_map/necf,efd->necd/dot_general | solution.py:194
  284.4 18.7 %reduce-scatter.3.cloned.1.call-done = bf16[32,4,8,1024]{3,2,0,1:T(8,128)(2,1)} async-done(((bf16[32,4,8,2048]{3,2,0,1:T(8,128)(2,1)}), bf16[32,4,8,1024]{3,2,0,1:T(8,128)(2,1)}) %reduce-scatter.3.cloned.1.call-update) | async-done | bytes 2097168 | tf_op jit(solution)/shard_map/reduce_scatter | solution.py:197
  303.1 35.9 %reduce-scatter.5.cloned.1.call-done = bf16[32,4,8,256]{3,2,0,1:T(8,128)(2,1)} async-done(((bf16[32,4,8,1024]{3,2,0,1:T(8,128)(2,1)}), bf16[32,4,8,256]{3,2,0,1:T(8,128)(2,1)}) %reduce-scatter.5.cloned.1.call-update) | async-done | bytes 524304 | tf_op jit(solution)/shard_map/reduce_scatter | solution.py:198
  339.1 1.9 copy.369
  341.0 10.1 %all-to-all-start.2 = ((bf16[32,32,256]{2,1,0:T(8,128)(2,1)}), bf16[32,32,256]{2,1,0:T(8,128)(2,1)}, u32[]{:S(2)}, u32[]{:S(2)}) async-start(bf16[32,32,256]{2,1,0:T(8,128)(2,1)} %bitcast.185), calls=%async_computation.4 | async-start | bytes 1048576 | tf_op jit(solution)/shard_map/all_to_all | solution.py:199
  351.4 17.3 %all-to-all-done.2 = bf16[32,32,256]{2,1,0:T(8,128)(2,1)} async-done(((bf16[32,32,256]{2,1,0:T(8,128)(2,1)}), bf16[32,32,256]{2,1,0:T(8,128)(2,1)}, u32[]{:S(2)}, u32[]{:S(2)}) %all-to-all-start.2) | async-done | bytes 524320 | tf_op jit(solution)/shard_map/all_to_all | solution.py:199
  369.8 2.2 gather_fusion
  372.1 1.9 fusion.58
  373.9 3.3 all-to-all-start.3
  377.3 5.4 %all-to-all-done.3 = bf16[8,8,256]{2,1,0:T(8,128)(2,1)S(1)} async-done(((bf16[8,8,256]{2,1,0:T(8,128)(2,1)}), bf16[8,8,256]{2,1,0:T(8,128)(2,1)S(1)}, u32[]{:S(2)}, u32[]{:S(2)}) %all-to-all-start.3) | async-done | bytes 32800 | tf_op jit(solution)/shard_map/all_to_all | solution.py:209
  (132 shorter events, 30.0 us)
Async XLA Ops:
  7.2 114.5 %copy-start = (bf16[512,2048]{1,0:T(8,128)(2,1)S(1)}, bf16[512,2048]{1,0:T(8,128)(2,1)}, u32[]{:S(2)}) copy-start(bf16[512,2048]{1,0:T(8,128)(2,1)} %param.24) | copy-start | bytes 6291460
  7.2 19.0 %copy-start.9 = (f32[128]{0:T(128)S(1)}, f32[128]{0:T(128)}, u32[]{:S(2)}) copy-start(f32[128]{0:T(128)} %param.23) | copy-start | bytes 1540
  7.2 18.4 %copy-start.10 = (f32[128]{0:T(128)S(1)}, f32[128]{0:T(128)}, u32[]{:S(2)}) copy-start(f32[128]{0:T(128)} %param.22) | copy-start | bytes 1540
  7.2 18.7 %copy-start.12 = (s32[2]{0:T(128)S(1)}, s32[2]{0:T(128)}, u32[]{:S(2)}) copy-start(s32[2]{0:T(128)} %param.33) | copy-start | bytes 28
  7.2 18.7 %copy-start.11 = (s32[64]{0:T(128)S(1)}, s32[64]{0:T(128)}, u32[]{:S(2)}) copy-start(s32[64]{0:T(128)} %param.35) | copy-start | bytes 772
  7.2 18.9 %copy-start.15 = (s32[64]{0:T(128)S(1)}, s32[64]{0:T(128)}, u32[]{:S(2)}) copy-start(s32[64]{0:T(128)} %param.34) | copy-start | bytes 772
  23.2 3.0 copy-start.13
  26.2 14.1 %copy-start.14 = (s32[2]{0:T(128)S(1)}, s32[2]{0:T(128)}, u32[]{:S(2)}) copy-start(s32[2]{0:T(128)} %copy-done.13) | copy-start | bytes 28
  26.4 13.8 %copy-start.6 = (bf16[64,128]{1,0:T(8,128)(2,1)}, bf16[64,128]{1,0:T(8,128)(2,1)S(1)}, u32[]{:S(2)}) copy-start(bf16[64,128]{1,0:T(8,128)(2,1)S(1)} %get-tuple-element.22) | copy-start | bytes 49156
  41.9 10.5 %copy-start.16 = (s32[64]{0:T(128)S(1)}, s32[64]{0:T(128)}, u32[]{:S(2)}) copy-start(s32[64]{0:T(128)} %param.34) | copy-start | bytes 772
  52.5 5.3 %copy-start.5 = (pred[64,16]{1,0:T(8,128)(4,1)}, pred[64,16]{1,0:T(8,128)(4,1)S(1)}, u32[]{:S(2)}) copy-start(pred[64,16]{1,0:T(8,128)(4,1)S(1)} %broadcast_compare_fusion) | copy-start | bytes 3076
  60.2 1.8 copy-start.4
  62.0 4.4 %copy-start.1 = (f32[4,64,8,2,256]{4,2,3,1,0:T(8,128)S(1)}, f32[4,64,8,2,256]{4,2,3,1,0:T(8,128)}, u32[]{:S(2)}) copy-start(f32[4,64,8,2,256]{4,2,3,1,0:T(8,128)} %get-tuple-element.29) | copy-start | bytes 12582916
  66.5 4.7 %copy-start.2 = (f32[64,4,8,16]{3,2,1,0:T(8,128)S(1)}, f32[64,4,8,16]{3,2,1,0:T(8,128)}, u32[]{:S(2)}) copy-start(f32[64,4,8,16]{3,2,1,0:T(8,128)} %get-tuple-element.31) | copy-start | bytes 393220
  80.3 7.8 %copy-start.8 = (s32[64,8]{0,1:T(8,128)S(1)}, s32[64,8]{0,1:T(8,128)}, u32[]{:S(2)}) copy-start(s32[64,8]{0,1:T(8,128)} %param.29) | copy-start | bytes 6148
  83.5 31.5 %all-to-all-start = ((f32[8,64,4,130]{3,1,2,0:T(8,128)}), f32[8,64,4,130]{3,1,2,0:T(8,128)}, u32[]{:S(2)}, u32[]{:S(2)}) async-start(f32[8,64,4,130]{3,1,2,0:T(8,128)} %maximum_bitcast_fusion), calls=%async_computation | async-start | bytes 4194304 | tf_op jit(solution)/shard_map/all_to_all | solution.py:155
  87.9 102.2 %all-reduce.2.cloned.1.call-start = ((), (), s32[]{:S(2)}) async-start(), calls=%async_computation.6 | async-start | bytes 1048576 | tf_op jit(solution)/shard_map/psum | solution.py:165
  123.1 128.1 %all-gather.3.cloned.1.call-start = ((), (), s32[]{:S(2)}) async-start(), calls=%async_computation.7 | async-start | bytes 2621440 | tf_op jit(solution)/shard_map/all_gather | solution.py:187
  191.3 0.7 copy-start.3
  218.0 55.0 %all-gather.5.cloned.1.call-start = ((), (), s32[]{:S(2)}) async-start(), calls=%async_computation.8 | async-start | bytes 6291456 | tf_op jit(solution)/shard_map/all_gather | solution.py:188
  251.2 51.9 %reduce-scatter.3.cloned.1.call-start = ((), (), s32[]{:S(2)}) async-start(), calls=%async_computation.9 | async-start | bytes 6291456 | tf_op jit(solution)/shard_map/reduce_scatter | solution.py:197
  284.3 67.0 %copy-start.7 = (f32[64,8]{0,1:T(8,128)S(1)}, f32[64,8]{0,1:T(8,128)}, u32[]{:S(2)}) copy-start(f32[64,8]{0,1:T(8,128)} %param.30) | copy-start | bytes 6148
  284.4 54.7 %reduce-scatter.5.cloned.1.call-start = ((), (), s32[]{:S(2)}) async-start(), calls=%async_computation.10 | async-start | bytes 2621440 | tf_op jit(solution)/shard_map/reduce_scatter | solution.py:198
  341.0 27.7 %all-to-all-start.2 = ((bf16[32,32,256]{2,1,0:T(8,128)(2,1)}), bf16[32,32,256]{2,1,0:T(8,128)(2,1)}, u32[]{:S(2)}, u32[]{:S(2)}) async-start(bf16[32,32,256]{2,1,0:T(8,128)(2,1)} %bitcast.185), calls=%async_computation.4 | async-start | bytes 1048576 | tf_op jit(solution)/shard_map/all_to_all | solution.py:199
  373.9 8.7 %all-to-all-start.3 = ((bf16[8,8,256]{2,1,0:T(8,128)(2,1)}), bf16[8,8,256]{2,1,0:T(8,128)(2,1)S(1)}, u32[]{:S(2)}, u32[]{:S(2)}) async-start(bf16[8,8,256]{2,1,0:T(8,128)(2,1)} %bitcast.163), calls=%async_computation.5 | async-start | bytes 65536 | tf_op jit(solution)/shard_map/all_to_all | solution.py:209
Sparse Core Ops, SparseCore 0:
  123.2 66.8 all-reduce.1
  218.1 33.0 all-gather.2
  253.0 19.9 all-gather.4
  284.5 18.5 reduce-scatter.2
  305.5 33.5 reduce-scatter.4
where the time goes:
time: 392 us; the launch traced here: 391 us
  waiting for transfers between devices  224 us (57%)
  blocking collectives  52.4 us (13%)
  matrix products  29.2 us (7%)
  local copies, waits for them, and re-layouts  27.5 us (7%)
  other arithmetic  25.3 us (6%)
  starting transfers between devices  18.2 us (5%)
  between operations  14.4 us (4%)
    psum x1, waiting for transfers between devices, body(): lax.psum(jnp.dot(attn_heads, out_weight, preferred_element_type=jnp.float...  65.4 us
    reduce_scatter x1, waiting for transfers between devices, body(): lax.psum_scatter(core_out, 'tx', scatter_dimension=3, tiled=True)  35.9 us
    all_gather x1, waiting for transfers between devices, body(): half_rows = lax.all_gather(arrived, 'tx', axis=2, tiled=True)  33.2 us
    all_to_all x1, waiting for transfers between devices, body(): parts = lax.all_to_all(packed, TENSOR, 0, 0, tiled=True)  25.8 us
    all_to_all x1, blocking collectives, body(): lax.all_to_all(outgoing, 'dp', split_axis=0, concat_axis=0, tiled=True)  25.5 us
    all_gather x1, waiting for transfers between devices, body(): lax.all_gather(half_rows, 'tc', axis=2, tiled=True)  21.8 us
    reduce_scatter x1, waiting for transfers between devices, body(): lax.psum_scatter(partial_out, 'tc', scatter_dimension=3, tiled=True)  18.7 us
    all_to_all x1, waiting for transfers between devices, body(): lax.all_to_all(summed_out.reshape(owners, local_experts * capacity, width...  17.3 us
  transfers between devices with their start and end apart: 8, of which 8 were waited for; matrix products, arithmetic and copies ran while one was open for 1% of the time, Pallas kernels for 0%

commit v1 on v0

--- a/solution.py
+++ b/solution.py
@@ -162,7 +162,10 @@
     sums_mine = jnp.sum(part_sums * factor[..., None], axis=0)
     mixed = sums_mine / total_mine[..., None]
     attn_heads = mixed.reshape(requests, query_cols).astype(jnp.bfloat16)
-    attn_all = lax.psum(jnp.dot(attn_heads, out_weight, preferred_element_type=jnp.float32), TENSOR)
+    attn_all = jnp.sum(
+        lax.all_gather(jnp.dot(attn_heads, out_weight, preferred_element_type=jnp.float32), TENSOR),
+        axis=0,
+    )
     middle_all = (residual_all.astype(jnp.float32) + attn_all).astype(jnp.bfloat16)
     tokens_here = residual_in.shape[0]
     middle = lax.dynamic_slice_in_dim(middle_all, tensor_rank * tokens_here, tokens_here, 0)

time: 392 us -> 359 us (0.916)
  waiting for transfers between devices: 224 us -> 163 us
  blocking collectives: 52.4 us -> 85.6 us
  starting transfers between devices: 18.2 us -> 13.7 us
    psum x1 -> x0, waiting for transfers between devices: 65.4 us -> none  [body(): lax.psum(jnp.dot(attn_heads, out_weight, preferred_element_type=jnp.float...]
    all_gather x0 -> x1, waiting for transfers between devices: none -> 32.7 us  [body(): lax.all_gather(jnp.dot(attn_heads, out_weight, preferred_element_type=jnp...]
    all_to_all x0 -> x1, blocking collectives: none -> 30.7 us  [body(): parts = lax.all_to_all(packed, TENSOR, 0, 0, tiled=True)]
    all_to_all x1 -> x0, waiting for transfers between devices: 25.8 us -> none  [body(): parts = lax.all_to_all(packed, TENSOR, 0, 0, tiled=True)]
    all_to_all x1 -> x0, starting transfers between devices: 4.34 us -> none  [body(): parts = lax.all_to_all(packed, TENSOR, 0, 0, tiled=True)]
    unnamed x42 -> x44, local copies, waits for them, and re-layouts: 8.87 us -> 9.58 us
  transfers between devices with their start and end apart: 8 -> 7, of which waited for: 8 -> 7; matrix products, arithmetic and copies ran while one was open for 1% -> 1% of each run, Pallas kernels for 0% -> 0%
where the time goes in v1:
time: 359 us; the launch traced here: 358 us
  waiting for transfers between devices  163 us (45%)
  blocking collectives  85.6 us (24%)
  matrix products  29.2 us (8%)
  local copies, waits for them, and re-layouts  28.3 us (8%)
  other arithmetic  23.9 us (7%)
  between operations  14.4 us (4%)
  starting transfers between devices  13.7 us (4%)
    reduce_scatter x1, waiting for transfers between devices, body(): lax.psum_scatter(core_out, 'tx', scatter_dimension=3, tiled=True)  35.9 us
    all_gather x1, waiting for transfers between devices, body(): lax.all_gather(jnp.dot(attn_heads, out_weight, preferred_element_type=jnp...  32.7 us
    all_gather x1, waiting for transfers between devices, body(): half_rows = lax.all_gather(arrived, 'tx', axis=2, tiled=True)  31.3 us
    all_to_all x1, blocking collectives, body(): parts = lax.all_to_all(packed, TENSOR, 0, 0, tiled=True)  30.7 us
    all_to_all x1, blocking collectives, body(): lax.all_to_all(outgoing, 'dp', split_axis=0, concat_axis=0, tiled=True)  28 us
    all_gather x1, waiting for transfers between devices, body(): lax.all_gather(half_rows, 'tc', axis=2, tiled=True)  21.8 us
    reduce_scatter x1, waiting for transfers between devices, body(): lax.psum_scatter(partial_out, 'tc', scatter_dimension=3, tiled=True)  18.7 us
    all_to_all x1, waiting for transfers between devices, body(): lax.all_to_all(summed_out.reshape(owners, local_experts * capacity, width...  17.3 us
  transfers between devices with their start and end apart: 7, of which 7 were waited for; matrix products, arithmetic and copies ran while one was open for 1% of the time, Pallas kernels for 0%

profile of v1, /device:TPU:32, one launch (start us, length us, event | category | flops | bytes accessed | tf_op | source)
XLA Modules:
  0.0 358.2 jit_solution(6526163685849980737)
XLA Ops:
  7.3 13.5 %all_gather.18 = bf16[64,2048]{1,0:T(8,128)(2,1)S(1)} all-gather(bf16[8,2048]{1,0:T(8,128)(2,1)} %param.18), channel_id=1, replica_groups=mesh['dp'=32,'tx'=4,'tc'=2] {'tx','tc'}, dimensions={0}, use_global_device_ids=true | all-gather | bytes 294912 | tf_op jit(solution)/shard_map/all_gather | solution.py:69
  23.3 2.1 fusion.80
  26.9 13.3 %all_gather.19 = bf16[64,5120]{1,0:T(8,128)(2,1)S(1)} all-gather(bf16[64,640]{1,0:T(8,128)(2,1)S(1)} %pad_maximum_fusion), channel_id=1, replica_groups=mesh['dp'=32,'tx'=4,'tc'=2] {'tx','tc'}, dimensions={1}, use_global_device_ids=true | all-gather | bytes 737280 | tf_op jit(solution)/shard_map/all_gather | solution.py:90
  42.0 2.1 fusion.107
  44.1 2.0 copy.307
  46.3 4.6 %fusion = (f32[64,4,8]{2,0,1:T(8,128)}, f32[4,64,8,2,256]{4,2,3,1,0:T(8,128)}) fusion(pred[64,2,256]{2,1,0:T(4,128)(4,1)S(1)} %broadcast_and_fusion, bf16[2,256,4,128,1]{1,3,2,0,4:T(8,128)(2,1)} %bitcast.195, bf16[64,4,8,128]{3,2,1,0:T(8,128)(2,1)S(1)} %reshape.329), kind=kOutput, calls=%fused_computation.3 | convolution fusion | flops 271579136 | bytes 5283840 | tf_op jit(solution)/shard_map/rgqd,npgd->rgqnp/dot_general | solution.py:106
  50.9 1.6 copy.257
  52.6 2.9 slice_bitcast_fusion
  55.5 2.4 select_reduce_fusion
  62.1 4.4 %fusion.7 = f32[64,4,8]{2,0,1:T(8,128)} fusion(f32[4,64,8,2,256]{4,2,3,1,0:T(8,128)} %get-tuple-element.29, f32[64,4,8]{2,0,1:T(8,128)S(1)} %copy.259, pred[64,2,256]{2,1,0:T(4,128)(4,1)S(1)} %broadcast_and_fusion), kind=kLoop, calls=%fused_computation.11 | loop fusion | flops 4192256 | bytes 4243456 | tf_op jit(solution)/shard_map/reduce_sum | solution.py:131
  66.5 3.2 fusion.19
  71.2 1.6 fusion.53
  72.8 2.0 fusion.22
  80.3 1.9 maximum_bitcast_fusion
  82.3 30.7 %all_to_all.25 = f32[8,64,4,130]{3,1,2,0:T(8,128)S(1)} all-to-all(f32[8,64,4,130]{3,1,2,0:T(8,128)S(1)} %maximum_bitcast_fusion), channel_id=1, replica_groups=mesh['dp'=32,'tx'=4,'tc'=2] {'tx','tc'}, dimensions={0} | all-to-all | bytes 2129920 | tf_op jit(solution)/shard_map/all_to_all | solution.py:155
  115.7 1.6 copy.310
  123.4 32.7 %all-gather.9.cloned.1.call-done = f32[512,2048]{1,0:T(8,128)} async-done(((f32[64,2048]{1,0:T(8,128)}), f32[512,2048]{1,0:T(8,128)}) %all-gather.9.cloned.1.call-update) | async-done | bytes 4194320 | tf_op jit(solution)/shard_map/all_gather | solution.py:166
  156.2 2.5 reduce_sum.125
  159.3 28.0 %all_to_all.26 = bf16[32,32,256]{2,1,0:T(8,128)(2,1)} all-to-all(bf16[32,32,256]{2,1,0:T(8,128)(2,1)S(1)} %bitcast.194), channel_id=1, replica_groups=mesh['dp'=32,'tx'=4,'tc'=2] {'dp'}, dimensions={0} | all-to-all | bytes 1048576 | tf_op jit(solution)/shard_map/all_to_all | solution.py:189
  187.4 31.3 %all-gather.5.cloned.1.call-done = bf16[32,32,1024]{2,1,0:T(8,128)(2,1)} async-done(((bf16[32,32,256]{2,1,0:T(8,128)(2,1)}), bf16[32,32,1024]{2,1,0:T(8,128)(2,1)}) %all-gather.5.cloned.1.call-update) | async-done | bytes 2097168 | tf_op jit(solution)/shard_map/all_gather | solution.py:190
  218.8 21.8 %all-gather.7.cloned.1.call-done = bf16[32,32,2048]{2,1,0:T(8,128)(2,1)} async-done(((bf16[32,32,1024]{2,1,0:T(8,128)(2,1)}), bf16[32,32,2048]{2,1,0:T(8,128)(2,1)}) %all-gather.7.cloned.1.call-update) | async-done | bytes 4194320 | tf_op jit(solution)/shard_map/all_gather | solution.py:191
  240.5 3.9 %fusion.23 = f32[32,4,8,96]{3,2,0,1:T(8,128)S(1)} fusion(bf16[4,2048,96]{1,2,0:T(8,128)(2,1)} %param.26, bf16[32,32,2048]{2,1,0:T(8,128)(2,1)} %all-gather.7.cloned.1.call-done), kind=kOutput, calls=%fused_computation.29 | convolution fusion | flops 402653184 | bytes 6160384 | tf_op jit(solution)/shard_map/necd,edf->necf/dot_general | solution.py:194
  244.5 7.4 %convert_bitcast_fusion = bf16[32,4,8,2048]{3,2,0,1:T(8,128)(2,1)} fusion(bf16[4,96,2048]{2,1,0:T(8,128)(2,1)} %param.28, bf16[4,2048,96]{1,2,0:T(8,128)(2,1)} %param.27, f32[32,4,8,96]{3,2,0,1:T(8,128)S(1)} %fusion.23, bf16[32,32,2048]{2,1,0:T(8,128)(2,1)} %all-gather.7.cloned.1.call-done), kind=kOutput, calls=%fused_computation.6 | convolution fusion | flops 807993344 | bytes 11927552 | tf_op jit(solution)/shard_map/necf,efd->necd/dot_general | solution.py:197
  251.9 18.7 %reduce-scatter.3.cloned.1.call-done = bf16[32,4,8,1024]{3,2,0,1:T(8,128)(2,1)} async-done(((bf16[32,4,8,2048]{3,2,0,1:T(8,128)(2,1)}), bf16[32,4,8,1024]{3,2,0,1:T(8,128)(2,1)}) %reduce-scatter.3.cloned.1.call-update) | async-done | bytes 2097168 | tf_op jit(solution)/shard_map/reduce_scatter | solution.py:200
  270.7 35.9 %reduce-scatter.5.cloned.1.call-done = bf16[32,4,8,256]{3,2,0,1:T(8,128)(2,1)} async-done(((bf16[32,4,8,1024]{3,2,0,1:T(8,128)(2,1)}), bf16[32,4,8,256]{3,2,0,1:T(8,128)(2,1)}) %reduce-scatter.5.cloned.1.call-update) | async-done | bytes 524304 | tf_op jit(solution)/shard_map/reduce_scatter | solution.py:201
  306.6 1.9 copy.368
  308.5 10.1 %all-to-all-start.2 = ((bf16[32,32,256]{2,1,0:T(8,128)(2,1)}), bf16[32,32,256]{2,1,0:T(8,128)(2,1)}, u32[]{:S(2)}, u32[]{:S(2)}) async-start(bf16[32,32,256]{2,1,0:T(8,128)(2,1)} %bitcast.185), calls=%async_computation.4 | async-start | bytes 1048576 | tf_op jit(solution)/shard_map/all_to_all | solution.py:202
  319.0 17.3 %all-to-all-done.2 = bf16[32,32,256]{2,1,0:T(8,128)(2,1)} async-done(((bf16[32,32,256]{2,1,0:T(8,128)(2,1)}), bf16[32,32,256]{2,1,0:T(8,128)(2,1)}, u32[]{:S(2)}, u32[]{:S(2)}) %all-to-all-start.2) | async-done | bytes 524320 | tf_op jit(solution)/shard_map/all_to_all | solution.py:202
  337.4 2.2 gather_fusion
  339.6 1.9 fusion.58
  341.5 3.3 all-to-all-start.3
  344.8 5.4 %all-to-all-done.3 = bf16[8,8,256]{2,1,0:T(8,128)(2,1)S(1)} async-done(((bf16[8,8,256]{2,1,0:T(8,128)(2,1)}), bf16[8,8,256]{2,1,0:T(8,128)(2,1)S(1)}, u32[]{:S(2)}, u32[]{:S(2)}) %all-to-all-start.3) | async-done | bytes 32800 | tf_op jit(solution)/shard_map/all_to_all | solution.py:212
  (135 shorter events, 29.3 us)
Async XLA Ops:
  7.2 112.2 %copy-start = (bf16[512,2048]{1,0:T(8,128)(2,1)S(1)}, bf16[512,2048]{1,0:T(8,128)(2,1)}, u32[]{:S(2)}) copy-start(bf16[512,2048]{1,0:T(8,128)(2,1)} %param.24) | copy-start | bytes 6291460
  7.2 19.1 %copy-start.10 = (f32[128]{0:T(128)S(1)}, f32[128]{0:T(128)}, u32[]{:S(2)}) copy-start(f32[128]{0:T(128)} %param.23) | copy-start | bytes 1540
  7.2 18.5 %copy-start.11 = (f32[128]{0:T(128)S(1)}, f32[128]{0:T(128)}, u32[]{:S(2)}) copy-start(f32[128]{0:T(128)} %param.22) | copy-start | bytes 1540
  7.2 18.7 %copy-start.13 = (s32[2]{0:T(128)S(1)}, s32[2]{0:T(128)}, u32[]{:S(2)}) copy-start(s32[2]{0:T(128)} %param.33) | copy-start | bytes 28
  7.2 18.7 %copy-start.12 = (s32[64]{0:T(128)S(1)}, s32[64]{0:T(128)}, u32[]{:S(2)}) copy-start(s32[64]{0:T(128)} %param.35) | copy-start | bytes 772
  7.2 18.9 %copy-start.16 = (s32[64]{0:T(128)S(1)}, s32[64]{0:T(128)}, u32[]{:S(2)}) copy-start(s32[64]{0:T(128)} %param.34) | copy-start | bytes 772
  7.2 148.9 %all-gather.9.cloned.1.call-start = ((), (), s32[]{:S(2)}) async-start(), calls=%async_computation.10 | async-start | bytes 4718592 | tf_op jit(solution)/shard_map/all_gather | solution.py:166
  23.3 3.0 copy-start.14
  26.3 14.1 %copy-start.15 = (s32[2]{0:T(128)S(1)}, s32[2]{0:T(128)}, u32[]{:S(2)}) copy-start(s32[2]{0:T(128)} %copy-done.14) | copy-start | bytes 28
  26.5 13.8 %copy-start.7 = (bf16[64,128]{1,0:T(8,128)(2,1)}, bf16[64,128]{1,0:T(8,128)(2,1)S(1)}, u32[]{:S(2)}) copy-start(bf16[64,128]{1,0:T(8,128)(2,1)S(1)} %get-tuple-element.22) | copy-start | bytes 49156
  42.0 10.5 %copy-start.17 = (s32[64]{0:T(128)S(1)}, s32[64]{0:T(128)}, u32[]{:S(2)}) copy-start(s32[64]{0:T(128)} %param.34) | copy-start | bytes 772
  52.5 5.3 %copy-start.6 = (pred[64,16]{1,0:T(8,128)(4,1)}, pred[64,16]{1,0:T(8,128)(4,1)S(1)}, u32[]{:S(2)}) copy-start(pred[64,16]{1,0:T(8,128)(4,1)S(1)} %broadcast_compare_fusion) | copy-start | bytes 3076
  60.3 1.8 copy-start.5
  62.1 4.4 %copy-start.1 = (f32[4,64,8,2,256]{4,2,3,1,0:T(8,128)S(1)}, f32[4,64,8,2,256]{4,2,3,1,0:T(8,128)}, u32[]{:S(2)}) copy-start(f32[4,64,8,2,256]{4,2,3,1,0:T(8,128)} %get-tuple-element.29) | copy-start | bytes 12582916
  66.5 4.7 %copy-start.3 = (f32[64,4,8,16]{3,2,1,0:T(8,128)S(1)}, f32[64,4,8,16]{3,2,1,0:T(8,128)}, u32[]{:S(2)}) copy-start(f32[64,4,8,16]{3,2,1,0:T(8,128)} %get-tuple-element.31) | copy-start | bytes 393220
  112.9 1.4 copy-start.2
  115.7 5.0 %copy-start.9 = (s32[64,8]{0,1:T(8,128)S(1)}, s32[64,8]{0,1:T(8,128)}, u32[]{:S(2)}) copy-start(s32[64,8]{0,1:T(8,128)} %param.29) | copy-start | bytes 6148
  120.7 98.0 %all-gather.5.cloned.1.call-start = ((), (), s32[]{:S(2)}) async-start(), calls=%async_computation.6 | async-start | bytes 2621440 | tf_op jit(solution)/shard_map/all_gather | solution.py:190
  158.8 85.6 %copy-start.4 = (bf16[64,2048]{1,0:T(8,128)(2,1)}, bf16[64,2048]{1,0:T(8,128)(2,1)S(1)}, u32[]{:S(2)}) copy-start(bf16[64,2048]{1,0:T(8,128)(2,1)S(1)} %get-tuple-element.5) | copy-start | bytes 786436
  187.3 53.2 %all-gather.7.cloned.1.call-start = ((), (), s32[]{:S(2)}) async-start(), calls=%async_computation.7 | async-start | bytes 6291456 | tf_op jit(solution)/shard_map/all_gather | solution.py:191
  218.7 52.0 %reduce-scatter.3.cloned.1.call-start = ((), (), s32[]{:S(2)}) async-start(), calls=%async_computation.8 | async-start | bytes 6291456 | tf_op jit(solution)/shard_map/reduce_scatter | solution.py:200
  251.9 67.0 %copy-start.8 = (f32[64,8]{0,1:T(8,128)S(1)}, f32[64,8]{0,1:T(8,128)}, u32[]{:S(2)}) copy-start(f32[64,8]{0,1:T(8,128)} %param.30) | copy-start | bytes 6148
  251.9 54.7 %reduce-scatter.5.cloned.1.call-start = ((), (), s32[]{:S(2)}) async-start(), calls=%async_computation.9 | async-start | bytes 2621440 | tf_op jit(solution)/shard_map/reduce_scatter | solution.py:201
  308.5 27.7 %all-to-all-start.2 = ((bf16[32,32,256]{2,1,0:T(8,128)(2,1)}), bf16[32,32,256]{2,1,0:T(8,128)(2,1)}, u32[]{:S(2)}, u32[]{:S(2)}) async-start(bf16[32,32,256]{2,1,0:T(8,128)(2,1)} %bitcast.185), calls=%async_computation.4 | async-start | bytes 1048576 | tf_op jit(solution)/shard_map/all_to_all | solution.py:202
  341.5 8.7 %all-to-all-start.3 = ((bf16[8,8,256]{2,1,0:T(8,128)(2,1)}), bf16[8,8,256]{2,1,0:T(8,128)(2,1)S(1)}, u32[]{:S(2)}, u32[]{:S(2)}) async-start(bf16[8,8,256]{2,1,0:T(8,128)(2,1)} %bitcast.163), calls=%async_computation.5 | async-start | bytes 65536 | tf_op jit(solution)/shard_map/all_to_all | solution.py:212
Sparse Core Ops, SparseCore 0:
  120.8 35.3 all-gather.8
  187.4 31.2 all-gather.4
  220.5 19.9 all-gather.6
  252.0 18.6 reduce-scatter.2
  273.1 33.5 reduce-scatter.4
